TPU v7x, 256 devices: a whole 4x4x8 slice. The times are simulated.
256 devices in a mesh: expert: 8 (over z_lo, core), tensor: 32 (over z_hi, x, y).
Axes of the slice: x: 4, y: 4, z: 8 (z_hi: 2, z_lo: 4; z = z_hi * 4 + z_lo), core: 2. Of those that a mesh axis runs over, the one named last changes fastest.
Arguments:
- tokens: bfloat16 [2048, 6144], P('expert', 'tensor'), may hold values from -6 to 6
- router_weight: bfloat16 [6144, 8], replicated, may hold values from -0.078125 to 0.078125
- expert_ids: int32 [2048, 2], P('expert'), may hold values from 0 to 7, all different within a row
- w_gate: bfloat16 [8, 6144, 8192], P('expert', None, 'tensor'), may hold values from -0.078125 to 0.078125
- w_up: bfloat16 [8, 6144, 8192], P('expert', None, 'tensor'), may hold values from -0.078125 to 0.078125
- w_down: bfloat16 [8, 8192, 6144], P('expert', 'tensor'), may hold values from -0.125 to 0.125
Outputs:
- moe_out: bfloat16 [2048, 6144], P('expert', 'tensor')
Inputs may be any that keep to these rules, and one draw needn't show every extreme that they name: `expert_ids`: each row names 2 different experts, and every expert is named by some row.
All inputs are finite; a program needn't handle non-finite values.
Results may differ from a plain program's by a relative error of at most 0.03.
Values may be sent and summed in bfloat16 or wider, within the bound.
No kernel may reach another device: no remote copies, remote signals or barrier semaphores. Data moves between devices by JAX's collectives and lax.ppermute only.
A program may use at most 64 MiB of HBM per device.

v0:
```python
import jax
import jax.numpy as jnp
from jax import lax
from jax.sharding import PartitionSpec as P


def body(tokens, router_weight, expert_ids, w_gate, w_up, w_down):
    tok_rows, part_width = tokens.shape
    top_count = expert_ids.shape[1]
    n_experts = lax.axis_size("expert")
    capacity = 5 * tok_rows * top_count // (4 * n_experts)
    slots_all = n_experts * capacity
    gate_local = w_gate[0]
    up_local = w_up[0]
    down_local = w_down[0]
    rows_count = n_experts * capacity
    flat_ids = expert_ids.reshape(-1)
    picks = tok_rows * top_count
    expert_hot = (flat_ids[:, None] == jnp.arange(n_experts, dtype=jnp.int32)[None, :]).astype(
        jnp.float32
    )
    lower = (jnp.arange(picks)[:, None] > jnp.arange(picks)[None, :]).astype(jnp.float32)
    before = jnp.dot(lower, expert_hot, precision=lax.Precision.HIGHEST)
    slot_pos = jnp.sum(before * expert_hot, axis=1).astype(jnp.int32)
    kept = slot_pos < capacity
    target = flat_ids * capacity + slot_pos
    placed = (target[:, None] == jnp.arange(slots_all, dtype=jnp.int32)[None, :]) & kept[:, None]
    placed = placed.reshape(tok_rows, top_count, slots_all).astype(jnp.float32)
    dispatch = jnp.sum(placed, axis=1).astype(jnp.bfloat16)
    contract_first = (((0,), (0,)), ((), ()))
    full_rows = lax.all_gather(tokens, "tensor", axis=1, tiled=True)
    logits = jnp.dot(full_rows, router_weight, preferred_element_type=jnp.float32)
    buckets = lax.dot_general(
        dispatch, full_rows, contract_first, preferred_element_type=jnp.float32
    ).astype(jnp.bfloat16)
    arrived = lax.all_to_all(
        buckets.reshape(n_experts, capacity, -1), "expert", split_axis=0, concat_axis=0, tiled=True
    )
    bucket_rows = arrived.reshape(rows_count, -1)
    gate = jnp.dot(bucket_rows, gate_local, preferred_element_type=jnp.float32)
    upper = jnp.dot(bucket_rows, up_local, preferred_element_type=jnp.float32)
    hidden = (jax.nn.silu(gate) * upper).astype(jnp.bfloat16)
    contract_hidden = (((0,), (1,)), ((), ()))
    summed = lax.psum_scatter(
        lax.dot_general(
            down_local, hidden, contract_hidden, preferred_element_type=jnp.float32
        ).astype(jnp.bfloat16),
        "tensor",
        scatter_dimension=0,
        tiled=True,
    )
    returned = lax.all_to_all(summed, "expert", split_axis=1, concat_axis=1, tiled=True)
    choose_hot = (
        expert_ids[:, :, None] == jnp.arange(n_experts, dtype=jnp.int32)[None, None, :]
    ).astype(jnp.float32)
    chosen = jnp.sum(choose_hot * logits[:, None, :], axis=2)
    weight = jax.nn.sigmoid(chosen - jnp.flip(chosen, axis=1)).astype(jnp.bfloat16)
    combine = jnp.sum(placed * weight.astype(jnp.float32)[:, :, None], axis=1).astype(jnp.bfloat16)
    mixed = lax.dot_general(
        combine, returned, (((1,), (1,)), ((), ())), preferred_element_type=jnp.float32
    )
    return mixed.astype(jnp.bfloat16)


def solution(mesh):
    in_specs = (
        P("expert", "tensor"),
        P(),
        P("expert", None),
        P("expert", None, "tensor"),
        P("expert", None, "tensor"),
        P("expert", "tensor", None),
    )
    out_specs = P("expert", "tensor")
    return jax.shard_map(body, mesh=mesh, in_specs=in_specs, out_specs=out_specs, check_vma=False)
```

profile of v0, /device:TPU:1, one launch (start us, length us, event | category | flops | bytes accessed | tf_op | source)
XLA Modules:
  0.0 633.0 jit_solution(9283036379071454045)
XLA Ops:
  6.5 0.0 copy-start
  6.5 0.0 copy-start.2
  6.5 0.0 all-gather.2.cloned.1.call-start
  6.5 0.7 all-gather.2.cloned.1.call-update
  7.3 0.0 reduce-scatter.4.cloned.1.call-start
  7.3 1.0 copy.26
  8.3 0.1 eq.42
  8.4 0.3 fusion.13
  8.7 0.1 convert_element_type.47
  8.9 0.1 copy.27
  8.9 0.7 multiply_add_fusion
  9.6 101.0 %all-gather.2.cloned.1.call-done = bf16[256,6144]{0,1:T(8,128)(2,1)} async-done(((bf16[256,192]{0,1:T(8,128)(2,1)}), bf16[256,6144]{0,1:T(8,128)(2,1)}) %all-gather.2.cloned.1.call-update) | async-done | bytes 3145744 | tf_op jit(solution)/shard_map/all_gather | solution.py:31
  110.6 2.4 fusion.22
  113.0 0.0 copy-done.2
  113.1 0.1 rev.4
  113.2 0.4 select_reduce_fusion
  113.6 4.2 convolution_convert_fusion.1
  117.8 0.0 copy-start.3
  117.8 179.8 %all_to_all.17 = bf16[8,80,6144]{2,1,0:T(8,128)(2,1)S(1)} all-to-all(bf16[8,80,6144]{2,1,0:T(8,128)(2,1)S(1)} %bitcast.30), channel_id=1, replica_groups=mesh['expert'=8,'tensor'=32] {'expert'}, dimensions={0} | all-to-all | bytes 15728640 | tf_op jit(solution)/shard_map/all_to_all | solution.py:36
  297.6 0.0 copy-start.1
  297.6 3.2 copy-done.1
  300.7 0.0 copy-done.3
  300.7 3.0 fusion.4
  303.8 0.0 copy-done
  303.8 16.6 %fusion = bf16[6144,640]{0,1:T(8,128)(2,1)} fusion(bf16[1,256,6144]{2,1,0:T(8,128)(2,1)S(1)} %copy-done, bf16[640,6144]{1,0:T(8,128)(2,1)} %bitcast.32, bf16[1,6144,256]{2,1,0:T(8,128)(2,1)} %param.10, f32[640,256]{1,0:T(8,128)} %fusion.4), kind=kOutput, calls=%fused_computation.2 | convolution fusion | flops 4031447040 | bytes 22675456 | tf_op jit(solution)/shard_map/dot_general | solution.py:45
  320.4 10.6 %copy.29 = bf16[6144,640]{1,0:T(8,128)(2,1)} copy(bf16[6144,640]{0,1:T(8,128)(2,1)} %fusion) | data formatting | bytes 15728640
  331.0 0.0 reduce-scatter.4.cloned.1.call-update
  331.0 274.8 %reduce-scatter.4.cloned.1.call-done = bf16[192,640]{1,0:T(8,128)(2,1)} async-done(((bf16[6144,640]{1,0:T(8,128)(2,1)}), bf16[192,640]{1,0:T(8,128)(2,1)}) %reduce-scatter.4.cloned.1.call-update) | async-done | bytes 245776
  605.8 1.8 copy.30
  607.7 17.5 %all_to_all.18 = bf16[192,8,80]{0,2,1:T(8,128)(2,1)S(1)} all-to-all(bf16[192,8,80]{0,2,1:T(8,128)(2,1)} %bitcast.34), channel_id=1, replica_groups=mesh['expert'=8,'tensor'=32] {'expert'}, dimensions={1} | all-to-all | bytes 491520 | tf_op jit(solution)/shard_map/all_to_all | solution.py:52
  625.2 1.0 convolution_convert_fusion.2
  (4 shorter events, 0.0 us)
Async XLA Ops:
  6.5 297.2 %copy-start = (bf16[1,256,6144]{2,1,0:T(8,128)(2,1)S(1)}, bf16[1,256,6144]{2,1,0:T(8,128)(2,1)}, u32[]{:S(2)}) copy-start(bf16[1,256,6144]{2,1,0:T(8,128)(2,1)} %param.11) | copy-start | bytes 9437188
  6.5 106.5 %copy-start.2 = (s32[256,2]{0,1:T(2,128)S(1)}, s32[256,2]{0,1:T(2,128)}, u32[]{:S(2)}) copy-start(s32[256,2]{0,1:T(2,128)} %param.8) | copy-start | bytes 6148
  6.5 104.1 %all-gather.2.cloned.1.call-start = ((), (), s32[]{:S(2)}) async-start(), calls=%async_computation.3 | async-start | bytes 3244032 | tf_op jit(solution)/shard_map/all_gather | solution.py:31
  7.3 598.6 %reduce-scatter.4.cloned.1.call-start = ((), (), s32[]{:S(2)}) async-start(), calls=%async_computation.4 | async-start | bytes 8110080
  117.8 183.0 %copy-start.3 = (bf16[1,6144,256]{2,1,0:T(8,128)(2,1)S(1)}, bf16[1,6144,256]{2,1,0:T(8,128)(2,1)}, u32[]{:S(2)}) copy-start(bf16[1,6144,256]{2,1,0:T(8,128)(2,1)} %param.9) | copy-start | bytes 9437188
  297.6 3.2 copy-start.1
Sparse Core Ops, SparseCore 0:
  10.7 99.8 all-gather.1
  331.1 274.6 reduce-scatter.3
where the time goes:
time: 633 us
  waiting for transfers between devices  377 us (60%)
  blocking collectives  197 us (31%)
  matrix products  27.4 us (4%)
  local copies, waits for them, and re-layouts  17 us (3%)
  between operations  13.5 us (2%)
    unnamed x3, waiting for transfers between devices  276 us
    all_to_all x1, blocking collectives, body(): lax.all_to_all(buckets.reshape(n_experts, capacity, -1), 'expert', split_...  180 us
    all_gather x1, waiting for transfers between devices, body(): full_rows = lax.all_gather(tokens, 'tensor', axis=1, tiled=True)  101 us
    all_to_all x1, blocking collectives, body(): lax.all_to_all(summed, 'expert', split_axis=1, concat_axis=1, tiled=True)  17.5 us
    dot_general x1, matrix products, body(): lax.dot_general(down_local, hidden, contract_hidden, preferred_element_ty...  16.6 us
    unnamed x11, local copies, waits for them, and re-layouts  16.6 us
  transfers between devices with their start and end apart: 2, of which 2 were waited for; matrix products, arithmetic and copies ran while one was open for 0% of the time, Pallas kernels for 0%

commit v1 on v0

--- a/solution.py
+++ b/solution.py
@@ -2,6 +2,11 @@
 import jax.numpy as jnp
 from jax import lax
 from jax.sharding import PartitionSpec as P
+
+
+def gather_over(shard, axis, along):
+    outgoing = jnp.stack([shard] * lax.axis_size(axis))
+    return jnp.concatenate(lax.all_to_all(outgoing, axis, 0, 0), axis=along)
 
 
 def body(tokens, router_weight, expert_ids, w_gate, w_up, w_down):
@@ -28,7 +33,7 @@
     placed = placed.reshape(tok_rows, top_count, slots_all).astype(jnp.float32)
     dispatch = jnp.sum(placed, axis=1).astype(jnp.bfloat16)
     contract_first = (((0,), (0,)), ((), ()))
-    full_rows = lax.all_gather(tokens, "tensor", axis=1, tiled=True)
+    full_rows = gather_over(tokens, "tensor", 1)
     logits = jnp.dot(full_rows, router_weight, preferred_element_type=jnp.float32)
     buckets = lax.dot_general(
         dispatch, full_rows, contract_first, preferred_element_type=jnp.float32

time: 633 us -> 618 us (0.976)
  waiting for transfers between devices: 377 us -> 324 us
  blocking collectives: 197 us -> 218 us
  starting transfers between devices: 0.04 us -> 14.8 us
    all_gather x1 -> x0, waiting for transfers between devices: 101 us -> none  [body(): full_rows = lax.all_gather(tokens, 'tensor', axis=1, tiled=True)]
    all_to_all x0 -> x1, waiting for transfers between devices: none -> 48.8 us  [gather_over(): return jnp.concatenate(lax.all_to_all(outgoing, axis, 0, 0), axis=along)]
    all_to_all x1, blocking collectives: 180 us -> 201 us  [body(): lax.all_to_all(buckets.reshape(n_experts, capacity, -1), 'expert', split_...]
    all_to_all x0 -> x1, starting transfers between devices: none -> 14.7 us  [gather_over(): return jnp.concatenate(lax.all_to_all(outgoing, axis, 0, 0), axis=along)]
    unnamed x11 -> x13, local copies, waits for them, and re-layouts: 16.6 us -> 15.8 us
    unnamed x3 -> x2, waiting for transfers between devices: 276 us -> 275 us
where the time goes in v1:
time: 618 us; the launch traced here: 617 us
  waiting for transfers between devices  324 us (52%)
  blocking collectives  218 us (35%)
  matrix products  27.4 us (4%)
  local copies, waits for them, and re-layouts  19.3 us (3%)
  starting transfers between devices  14.8 us (2%)
  between operations  13.5 us (2%)
    unnamed x2, waiting for transfers between devices  275 us
    all_to_all x1, blocking collectives, body(): lax.all_to_all(buckets.reshape(n_experts, capacity, -1), 'expert', split_...  201 us
    all_to_all x1, waiting for transfers between devices, gather_over(): return jnp.concatenate(lax.all_to_all(outgoing, axis, 0, 0), axis=along)  48.8 us
    all_to_all x1, blocking collectives, body(): lax.all_to_all(summed, 'expert', split_axis=1, concat_axis=1, tiled=True)  17.5 us
    dot_general x1, matrix products, body(): lax.dot_general(down_local, hidden, contract_hidden, preferred_element_ty...  16.6 us
    unnamed x13, local copies, waits for them, and re-layouts  15.8 us
    all_to_all x1, starting transfers between devices, gather_over(): return jnp.concatenate(lax.all_to_all(outgoing, axis, 0, 0), axis=along)  14.7 us
  transfers between devices with their start and end apart: 2, of which 2 were waited for; matrix products, arithmetic and copies ran while one was open for 0% of the time, Pallas kernels for 0%

profile of v1, /device:TPU:1, one launch (start us, length us, event | category | flops | bytes accessed | tf_op | source)
XLA Modules:
  0.0 617.4 jit_solution(6173137816769787662)
XLA Ops:
  6.5 0.0 copy-start
  6.5 3.1 stack.2
  9.6 0.0 copy-start.3
  9.6 0.0 copy-start.2
  9.6 14.7 %all-to-all-start = ((bf16[32,256,192]{1,2,0:T(8,128)(2,1)}), bf16[32,256,192]{1,2,0:T(8,128)(2,1)}, u32[]{:S(2)}, u32[]{:S(2)}) async-start(bf16[32,256,192]{1,2,0:T(8,128)(2,1)} %stack.2), calls=%async_computation | async-start | bytes 6291456 | tf_op jit(solution)/shard_map/all_to_all | solution.py:9
  24.4 0.0 reduce-scatter.4.cloned.1.call-start
  24.4 0.0 copy-done.3
  24.4 0.1 copy.27
  24.6 0.1 eq.42
  24.7 0.3 fusion.13
  25.0 0.1 convert_element_type.47
  25.2 0.1 copy.28
  25.2 48.8 %all-to-all-done = bf16[32,256,192]{1,2,0:T(8,128)(2,1)} async-done(((bf16[32,256,192]{1,2,0:T(8,128)(2,1)}), bf16[32,256,192]{1,2,0:T(8,128)(2,1)}, u32[]{:S(2)}, u32[]{:S(2)}) %all-to-all-start) | async-done | bytes 3145760 | tf_op jit(solution)/shard_map/all_to_all | solution.py:9
  74.1 0.0 copy-done.2
  74.1 2.4 fusion.22
  76.5 0.1 rev.4
  76.6 0.4 select_reduce_fusion
  77.0 4.2 convolution_convert_fusion.1
  81.2 0.0 copy-start.4
  81.2 200.7 %all_to_all.22 = bf16[8,80,6144]{2,1,0:T(8,128)(2,1)S(1)} all-to-all(bf16[8,80,6144]{2,1,0:T(8,128)(2,1)S(1)} %bitcast.33), channel_id=1, replica_groups=mesh['expert'=8,'tensor'=32] {'expert'}, dimensions={0} | all-to-all | bytes 15728640 | tf_op jit(solution)/shard_map/all_to_all | solution.py:41
  281.9 0.0 copy-start.1
  281.9 3.2 copy-done.1
  285.1 0.0 copy-done.4
  285.1 3.0 fusion.4
  288.1 0.0 copy-done
  288.1 16.6 %fusion = bf16[6144,640]{0,1:T(8,128)(2,1)} fusion(bf16[1,256,6144]{2,1,0:T(8,128)(2,1)S(1)} %copy-done, bf16[640,6144]{1,0:T(8,128)(2,1)} %bitcast.35, bf16[1,6144,256]{2,1,0:T(8,128)(2,1)} %param.10, f32[640,256]{1,0:T(8,128)} %fusion.4), kind=kOutput, calls=%fused_computation.2 | convolution fusion | flops 4031447040 | bytes 22675456 | tf_op jit(solution)/shard_map/dot_general | solution.py:50
  304.7 10.6 %copy.30 = bf16[6144,640]{1,0:T(8,128)(2,1)} copy(bf16[6144,640]{0,1:T(8,128)(2,1)} %fusion) | data formatting | bytes 15728640
  315.4 0.0 reduce-scatter.4.cloned.1.call-update
  315.4 274.8 %reduce-scatter.4.cloned.1.call-done = bf16[192,640]{1,0:T(8,128)(2,1)} async-done(((bf16[6144,640]{1,0:T(8,128)(2,1)}), bf16[192,640]{1,0:T(8,128)(2,1)}) %reduce-scatter.4.cloned.1.call-update) | async-done | bytes 245776
  590.2 1.8 copy.31
  592.0 17.5 %all_to_all.23 = bf16[192,8,80]{0,2,1:T(8,128)(2,1)S(1)} all-to-all(bf16[192,8,80]{0,2,1:T(8,128)(2,1)} %bitcast.37), channel_id=1, replica_groups=mesh['expert'=8,'tensor'=32] {'expert'}, dimensions={1} | all-to-all | bytes 491520 | tf_op jit(solution)/shard_map/all_to_all | solution.py:57
  609.6 1.0 convolution_convert_fusion.2
  (5 shorter events, 0.0 us)
Async XLA Ops:
  6.5 281.6 %copy-start = (bf16[1,256,6144]{2,1,0:T(8,128)(2,1)S(1)}, bf16[1,256,6144]{2,1,0:T(8,128)(2,1)}, u32[]{:S(2)}) copy-start(bf16[1,256,6144]{2,1,0:T(8,128)(2,1)} %param.11) | copy-start | bytes 9437188
  9.6 14.8 %copy-start.3 = (s32[256,2]{0,1:T(2,128)S(1)}, s32[256,2]{0,1:T(2,128)}, u32[]{:S(2)}) copy-start(s32[256,2]{0,1:T(2,128)} %param.8) | copy-start | bytes 6148
  9.6 64.4 %copy-start.2 = (bf16[6144,8]{0,1:T(8,128)(2,1)S(1)}, bf16[6144,8]{0,1:T(8,128)(2,1)}, u32[]{:S(2)}) copy-start(bf16[6144,8]{0,1:T(8,128)(2,1)} %param.7) | copy-start | bytes 294916
  9.6 64.4 %all-to-all-start = ((bf16[32,256,192]{1,2,0:T(8,128)(2,1)}), bf16[32,256,192]{1,2,0:T(8,128)(2,1)}, u32[]{:S(2)}, u32[]{:S(2)}) async-start(bf16[32,256,192]{1,2,0:T(8,128)(2,1)} %stack.2), calls=%async_computation | async-start | bytes 6291456 | tf_op jit(solution)/shard_map/all_to_all | solution.py:9
  24.4 565.8 %reduce-scatter.4.cloned.1.call-start = ((), (), s32[]{:S(2)}) async-start(), calls=%async_computation.4 | async-start | bytes 8110080
  81.2 203.9 %copy-start.4 = (bf16[1,6144,256]{2,1,0:T(8,128)(2,1)S(1)}, bf16[1,6144,256]{2,1,0:T(8,128)(2,1)}, u32[]{:S(2)}) copy-start(bf16[1,6144,256]{2,1,0:T(8,128)(2,1)} %param.9) | copy-start | bytes 9437188
  281.9 3.2 copy-start.1
Sparse Core Ops, SparseCore 0:
  315.5 274.6 reduce-scatter.3
